TPU v7x, 256 devices: a whole 4x4x8 slice. The times are simulated.
256 devices in a mesh: req: 64 (over z, x, core), tp: 4 (over y).
Axes of the slice: x: 4, y: 4, z: 8, core: 2. Of those that a mesh axis runs over, the one named last changes fastest.
Arguments:
- hidden: bfloat16 [16384, 2048], P('req'), may hold values from -10.5 to 10.5
- lengths: int32 [64], replicated, may hold values from 1 to 1024, 16384 in all
- dealing: int32 [64], replicated, may hold values from 0 to 63, each once
- norm_gain: bfloat16 [2048], replicated, may hold values from 0.5 to 1.5
- w_query: bfloat16 [2048, 2048], P(None, 'tp'), may hold values from -0.125 to 0.125
- w_key: bfloat16 [2048, 1024], P(None, 'tp'), may hold values from -0.125 to 0.125
- w_value: bfloat16 [2048, 1024], P(None, 'tp'), may hold values from -0.125 to 0.125
- query_gain: bfloat16 [128], replicated, may hold values from 0.5 to 8
- key_gain: bfloat16 [128], replicated, may hold values from 0.5 to 8
- w_out: bfloat16 [2048, 2048], P(None, 'tp'), may hold values from -0.125 to 0.125
Outputs:
- hidden_out: bfloat16 [16384, 2048], P('req', 'tp')
- kv_cache: bfloat16 [2, 64, 1024, 1024], P(None, 'req', None, 'tp')
Inputs may be any that keep to these rules, and one draw needn't show every extreme that they name: The lengths sum to 16384; the largest is exactly 1024. A permutation: dealt slot j, on device j of req, holds prompt dealing[j].
All inputs are finite; a program needn't handle non-finite values.
Results may differ from a plain program's by a relative error of at most 0.012.
The roundings to bfloat16 on the way count: a program that leaves them out, or rounds other values in their place, can miss the bound.
Values may be sent and summed in bfloat16 or wider, within the bound.
No kernel may reach another device: no remote copies, remote signals or barrier semaphores. Data moves between devices by JAX's collectives and lax.ppermute only.
A program may use at most 128 MiB of HBM per device.

v0:
```python
import jax
import jax.numpy as jnp
from jax import lax
from jax.sharding import PartitionSpec as P

EPS = 1e-06
THETA = 1000000.0


def rms_rows(values, scale_gain):
    inv_rms = lax.rsqrt(jnp.mean(values * values, axis=-1, keepdims=True) + EPS)
    return values * inv_rms * scale_gain


def rotate(values, positions):
    features = values.shape[-1]
    half_width = features // 2
    frequency = THETA ** (-(jnp.arange(half_width).astype(jnp.float32) * 2.0) / features)
    angles = positions.astype(jnp.float32)[:, None] * frequency[None, :]
    cosine = jnp.cos(angles)[:, None, :]
    sine_part = jnp.sin(angles)[:, None, :]
    first_half = values[..., :half_width]
    second_half = values[..., half_width:]
    return jnp.concatenate(
        [
            first_half * cosine - second_half * sine_part,
            second_half * cosine + first_half * sine_part,
        ],
        axis=-1,
    )


def project(normed, w_query, w_key, w_value, query_gain, key_gain, positions):
    head_dim = query_gain.shape[0]
    row_count = normed.shape[0]
    query_rows = jnp.dot(normed, w_query, preferred_element_type=jnp.float32).reshape(
        row_count, -1, head_dim
    )
    key_rows = jnp.dot(normed, w_key, preferred_element_type=jnp.float32).reshape(
        row_count, -1, head_dim
    )
    value_rows = jnp.dot(normed, w_value, preferred_element_type=jnp.float32).astype(jnp.bfloat16)
    query_rows = rotate(rms_rows(query_rows, query_gain.astype(jnp.float32)), positions).astype(
        jnp.bfloat16
    )
    key_rows = rotate(rms_rows(key_rows, key_gain.astype(jnp.float32)), positions).astype(
        jnp.bfloat16
    )
    return (query_rows.reshape(row_count, -1), key_rows.reshape(row_count, -1), value_rows)


def attend(query_slot, key_slot, value_slot, prompt_length, head_dim):
    slot_len, query_width = query_slot.shape
    kv_heads = key_slot.shape[1] // head_dim
    group_size = query_width // head_dim // kv_heads
    queries = query_slot.reshape(slot_len, kv_heads, group_size, head_dim)
    keys_split = key_slot.reshape(slot_len, kv_heads, head_dim)
    values_split = value_slot.reshape(slot_len, kv_heads, head_dim)
    scores = jnp.einsum(
        "qkgd,skd->kgqs", queries, keys_split, preferred_element_type=jnp.float32
    ) * head_dim ** (-0.5)
    offsets = jnp.arange(slot_len, dtype=jnp.int32)
    allowed = (offsets[None, :] <= offsets[:, None]) & (offsets[None, :] < prompt_length)
    scores = jnp.where(allowed[None, None], scores, -jnp.inf)
    row_max = jnp.max(scores, axis=-1, keepdims=True)
    weights = jnp.exp(scores - row_max)
    weights = (weights / jnp.sum(weights, axis=-1, keepdims=True)).astype(jnp.bfloat16)
    mixture = jnp.einsum(
        "kgqs,skd->qkgd", weights, values_split, preferred_element_type=jnp.float32
    )
    return mixture.astype(jnp.bfloat16).reshape(slot_len, query_width)


def on_device(
    hidden, lengths, dealing, norm_gain, w_query, w_key, w_value, query_gain, key_gain, w_out
):
    devices = lax.axis_size("req")
    home_index = lax.axis_index("req")
    slice_index = lax.axis_index("tp")
    tok_rows, features = hidden.shape
    head_dim = query_gain.shape[0]
    out_width = w_out.shape[1]
    q_width = w_query.shape[1]
    k_width = w_key.shape[1]
    slot_len = 4 * tok_rows
    capacity = slot_len // devices
    prompt_total = lengths.shape[0]
    prompt_ids = jnp.arange(prompt_total, dtype=jnp.int32)
    prompt_ends = jnp.cumsum(lengths)
    starts = prompt_ends - lengths
    packed_ids = jnp.arange(tok_rows, dtype=jnp.int32) * devices + home_index
    segment = jnp.sum((packed_ids[:, None] >= prompt_ends[None, :]).astype(jnp.int32), axis=1)
    seg_onehot = (segment[:, None] == prompt_ids[None, :]).astype(jnp.int32)
    positions = packed_ids - jnp.sum(seg_onehot * starts[None, :], axis=1)
    inverse = jnp.zeros((prompt_total,), jnp.int32).at[dealing].set(prompt_ids)
    deal_hot = (dealing[:, None] == prompt_ids[None, :]).astype(jnp.int32)
    dealt_starts = jnp.sum(deal_hot * starts[None, :], axis=1)
    dealt_lengths = jnp.sum(deal_hot * lengths[None, :], axis=1)
    first_offset = jnp.mod(home_index - dealt_starts, devices)
    ranks = jnp.arange(capacity, dtype=jnp.int32)
    slot_offset = first_offset[None, :] + ranks[:, None] * devices
    send_valid = slot_offset < dealt_lengths[None, :]
    send_rows = jnp.where(
        send_valid, (dealt_starts[None, :] + slot_offset - home_index) // devices, 0
    ).reshape(-1)
    my_start = lax.dynamic_index_in_dim(dealt_starts, home_index, 0, keepdims=False)
    my_length = lax.dynamic_index_in_dim(dealt_lengths, home_index, 0, keepdims=False)
    roll_shift = jnp.mod(my_start, devices)
    my_slots = jnp.sum(seg_onehot * inverse[None, :], axis=1)
    back_rows = positions // devices * devices + my_slots
    gain_values = norm_gain.astype(jnp.float32)
    normed = rms_rows(hidden.astype(jnp.float32), gain_values).astype(jnp.bfloat16)
    query_rows, key_rows, value_rows = project(
        normed, w_query, w_key, w_value, query_gain, key_gain, positions
    )
    qkv_rows = jnp.concatenate([query_rows, key_rows, value_rows], axis=1)
    picked = jnp.take(qkv_rows, send_rows, axis=0).reshape(capacity, devices, qkv_rows.shape[1])
    arrived = lax.all_to_all(
        jnp.where(send_valid[:, :, None], picked, jnp.zeros((), qkv_rows.dtype)),
        "req",
        split_axis=1,
        concat_axis=1,
        tiled=True,
    )
    slot_rows = jnp.roll(arrived, -roll_shift, axis=1).reshape(slot_len, arrived.shape[2])
    query_slot = slot_rows[:, :q_width]
    key_slot = slot_rows[:, q_width : q_width + k_width]
    value_slot = slot_rows[:, q_width + k_width :]
    mixture = attend(query_slot, key_slot, value_slot, my_length, head_dim)
    sendback = jnp.roll(mixture.reshape(capacity, devices, mixture.shape[1]), roll_shift, axis=1)
    returned = lax.all_to_all(sendback, "req", split_axis=1, concat_axis=1, tiled=True)
    attended = jnp.take(returned.reshape(capacity * devices, -1), back_rows, axis=0)
    kv_cache = jnp.stack([key_slot, value_slot])[:, None]
    summed = jnp.dot(
        lax.all_gather(attended, "tp", axis=1, tiled=True),
        w_out,
        preferred_element_type=jnp.float32,
    )
    branch = lax.optimization_barrier(summed.astype(jnp.bfloat16))
    residual = lax.dynamic_slice_in_dim(hidden, slice_index * out_width, out_width, 1)
    hidden_out = (residual.astype(jnp.float32) + branch.astype(jnp.float32)).astype(jnp.bfloat16)
    return (hidden_out, kv_cache)


def solution(mesh):
    in_specs = (
        P("req", None),
        P(),
        P(),
        P(),
        P(None, "tp"),
        P(None, "tp"),
        P(None, "tp"),
        P(),
        P(),
        P(None, "tp"),
    )
    out_specs = (P("req", "tp"), P(None, "req", None, "tp"))
    return jax.shard_map(
        on_device, mesh=mesh, in_specs=in_specs, out_specs=out_specs, check_vma=False
    )
```

profile of v0, /device:TPU:2, one launch (start us, length us, event | category | flops | bytes accessed | tf_op | source)
XLA Modules:
  0.0 212.4 jit_solution(9252795499204256088)
XLA Ops:
  7.2 0.9 copy.123
  8.1 0.1 reduce-window.8
  8.2 0.1 reduce
  8.3 0.7 sub.88
  9.0 0.8 select_reduce_fusion.2
  9.8 0.7 compare_select_fusion.7
  10.5 0.1 fusion.17
  10.6 0.6 compare_and_fusion
  11.2 0.7 lt.124
  11.9 0.1 copy.124
  12.0 0.7 convert_element_type.73
  12.7 1.6 fusion.7
  14.3 2.2 %convolution_convert_fusion.1 = bf16[256,256]{0,1:T(8,128)(2,1)S(1)} fusion(bf16[2048,256]{1,0:T(8,128)(2,1)} %param.16, bf16[256,2048]{1,0:T(8,128)(2,1)} %param.10, f32[2048]{0:T(1024)S(1)} %convert_element_type.73, f32[256]{0:T(256)S(1)} %add_rsqrt_fusion.2), kind=kOutput, calls=%fused_computation.30 | convolution fusion | flops 270598144 | bytes 2237440 | tf_op jit(solution)/shard_map/dot_general | solution.py:42
  16.6 0.7 copy.131
  17.3 0.6 convert_element_type.79
  17.9 2.6 %multiply_reduce_fusion.1 = (f32[256,2]{0,1:T(2,128)S(1)}, f32[256,256]{0,1:T(8,128)}) fusion(bf16[2048,256]{1,0:T(8,128)(2,1)} %param.15, bf16[256,2048]{1,0:T(8,128)(2,1)S(1)} %copy-done.1, f32[2048]{0:T(1024)S(1)} %convert_element_type.73, f32[256]{0:T(256)S(1)} %add_rsqrt_fusion.2), kind=kOutput, calls=%fused_computation.42 | convolution fusion | flops 270663168 | bytes 2370560 | tf_op jit(solution)/shard_map/dot_general | solution.py:39
  20.5 0.6 add_rsqrt_fusion.1
  21.0 0.1 convert_reduce_fusion
  21.1 0.8 scatter_custom_fusion
  21.9 0.6 select_reduce_fusion
  22.6 0.6 copy-done.5
  23.1 0.3 multiply_cosine_fusion
  23.5 0.1 copy.129
  23.6 0.1 copy.128
  23.7 1.1 multiply_multiply_fusion.1
  24.8 0.8 copy.149
  25.6 2.3 %fusion.29 = f32[256,512]{1,0:T(8,128)} fusion(bf16[2048,512]{1,0:T(8,128)(2,1)S(1)} %copy-done, bf16[256,2048]{1,0:T(8,128)(2,1)S(1)} %copy-done.1, f32[2048]{0:T(1024)} %copy-done.9, f32[256]{0:T(256)} %copy-done.14), kind=kOutput, calls=%fused_computation.107 | convolution fusion | flops 538968064 | bytes 3679232 | tf_op jit(solution)/shard_map/dot_general | solution.py:36
  27.8 1.2 reshape.456
  29.1 0.3 multiply_reduce_fusion
  29.5 0.3 multiply_multiply_fusion
  29.8 0.5 subtract_convert_fusion
  30.3 0.4 pad_maximum_fusion.1
  30.7 0.1 sub.98
  30.9 0.1 copy.125
  31.1 5.4 %gather_fusion = bf16[1024,1024]{1,0:T(8,128)(2,1)} fusion(bf16[256,1024]{1,0:T(8,128)(2,1)S(1)} %pad_maximum_fusion, s32[1024]{0:T(1024)S(1)} %broadcast_clamp_fusion), kind=kCustom, calls=%fused_computation | custom fusion | bytes 4198400 | tf_op jit(solution)/shard_map/jit(_take)/gather | solution.py:117
  36.5 4.0 %fusion.11 = bf16[16,64,1024]{2,0,1:T(8,128)(2,1)} fusion(bf16[16,64,1024]{2,1,0:T(8,128)(2,1)} %bitcast.61, pred[16,64]{0,1:T(8,128)(4,1)S(1)} %copy.125, pred[16,64]{0,1:T(8,128)(4,1)S(1)} %copy.124), kind=kLoop, calls=%fused_computation.25 | loop fusion | flops 2097152 | bytes 4196352 | tf_op jit(solution)/shard_map/jit(_where)/select_n | solution.py:119
  40.5 12.4 %all-to-all-start = ((bf16[16,64,1024]{2,0,1:T(8,128)(2,1)}), bf16[16,64,1024]{2,0,1:T(8,128)(2,1)}, u32[]{:S(2)}, u32[]{:S(2)}) async-start(bf16[16,64,1024]{2,0,1:T(8,128)(2,1)} %fusion.11), calls=%async_computation | async-start | bytes 4194304 | tf_op jit(solution)/shard_map/all_to_all | solution.py:118
  52.9 0.6 dynamic_slice.19
  55.5 0.6 dynamic_slice.21
  56.1 0.6 iota_compare_fusion.3
  56.7 1.3 fusion.6
  58.0 46.0 %all-to-all-done = bf16[16,64,1024]{2,0,1:T(8,128)(2,1)} async-done(((bf16[16,64,1024]{2,0,1:T(8,128)(2,1)}), bf16[16,64,1024]{2,0,1:T(8,128)(2,1)}, u32[]{:S(2)}, u32[]{:S(2)}) %all-to-all-start) | async-done | bytes 2097184 | tf_op jit(solution)/shard_map/all_to_all | solution.py:118
  104.0 2.7 %copy.133 = bf16[16,64,1024]{2,1,0:T(8,128)(2,1)S(1)} copy(bf16[16,64,1024]{2,0,1:T(8,128)(2,1)} %all-to-all-done) | data formatting | bytes 4194304 | tf_op jit(solution)/shard_map/all_to_all | solution.py:118
  106.8 1.6 fusion.10
  108.4 1.4 slice_bitcast_fusion
  109.8 0.1 slice.38
  109.9 2.0 copy.135
  112.0 2.1 copy.136
  114.0 1.3 copy.137
  115.3 11.2 %fusion.31 = (f32[2,2,1024]{2,1,0:T(2,128)S(1)}, f32[2,2,1024,1024]{2,3,1,0:T(8,128)}) fusion(pred[1024,1024]{0,1:T(8,128)(4,1)} %fusion.6, bf16[1024,2,128,1]{0,2,3,1:T(8,128)(2,1)} %bitcast.68, bf16[1024,2,2,128]{0,3,2,1:T(8,128)(2,1)} %bitcast.65), kind=kOutput, calls=%fused_computation.108 | convolution fusion | flops 1090520064 | bytes 19415040 | tf_op jit(solution)/shard_map/sub | solution.py:66
  126.5 7.2 %fusion.15 = bf16[1024,2,2,128]{0,3,2,1:T(8,128)(2,1)S(1)} fusion(bf16[1024,2,128,1]{0,2,3,1:T(8,128)(2,1)} %bitcast.67, f32[2,2,1024,1024]{2,3,1,0:T(8,128)} %get-tuple-element.35, f32[2,2,1024]{2,1,0:T(2,128)S(1)} %get-tuple-element.34), kind=kOutput, calls=%fused_computation.28 | convolution fusion | flops 1082654720 | bytes 18366464 | tf_op jit(solution)/shard_map/kgqs,skd->qkgd/dot_general | solution.py:68
  133.8 2.0 copy.141
  135.8 1.5 reshape_reshape.3
  137.3 0.8 fusion.16
  138.1 1.5 copy.142
  139.7 5.6 %all-to-all-start.1 = ((bf16[16,64,512]{2,0,1:T(8,128)(2,1)}), bf16[16,64,512]{2,0,1:T(8,128)(2,1)}, u32[]{:S(2)}, u32[]{:S(2)}) async-start(bf16[16,64,512]{2,0,1:T(8,128)(2,1)} %copy.142), calls=%async_computation.1 | async-start | bytes 2097152 | tf_op jit(solution)/shard_map/all_to_all | solution.py:131
  145.4 28.6 %all-to-all-done.1 = bf16[16,64,512]{2,0,1:T(8,128)(2,1)} async-done(((bf16[16,64,512]{2,0,1:T(8,128)(2,1)}), bf16[16,64,512]{2,0,1:T(8,128)(2,1)}, u32[]{:S(2)}, u32[]{:S(2)}) %all-to-all-start.1) | async-done | bytes 1048608 | tf_op jit(solution)/shard_map/all_to_all | solution.py:131
  174.0 1.8 copy.143
  175.8 1.2 gather_fusion.1
  176.9 0.8 broadcast_select_fusion
  177.8 2.3 %maximum_bitcast_fusion = bf16[2,1,1024,256]{3,2,1,0:T(8,128)(2,1)} fusion(bf16[1,1024,256]{2,1,0:T(8,128)(2,1)} %get-tuple-element.21, bf16[1,1024,256]{2,1,0:T(8,128)(2,1)} %get-tuple-element.20), kind=kLoop, calls=%fused_computation.32 | loop fusion | flops 524288 | bytes 2097152
  180.1 21.2 %all-gather.2.cloned.1.call-done = bf16[256,2048]{1,0:T(8,128)(2,1)} async-done(((bf16[256,512]{1,0:T(8,128)(2,1)}), bf16[256,2048]{1,0:T(8,128)(2,1)}) %all-gather.2.cloned.1.call-update) | async-done | bytes 1048592 | tf_op jit(solution)/shard_map/all_gather | solution.py:135
  201.2 2.6 %convolution_convert_fusion = bf16[256,512]{1,0:T(8,128)(2,1)S(1)} fusion(bf16[256,2048]{1,0:T(8,128)(2,1)} %all-gather.2.cloned.1.call-done, bf16[2048,512]{1,0:T(8,128)(2,1)} %param.19), kind=kOutput, calls=%fused_computation.29 | convolution fusion | flops 537001984 | bytes 3407872 | tf_op jit(solution)/shard_map/dot_general | solution.py:134
  203.8 1.7 add_convert_fusion
  (52 shorter events, 0.4 us)
Async XLA Ops:
  7.2 18.4 %copy-start = (bf16[2048,512]{1,0:T(8,128)(2,1)S(1)}, bf16[2048,512]{1,0:T(8,128)(2,1)}, u32[]{:S(2)}) copy-start(bf16[2048,512]{1,0:T(8,128)(2,1)} %param.14) | copy-start | bytes 6291460
  9.8 2.2 %copy-start.10 = (s32[64]{0:T(128)}, s32[64]{0:T(128)S(1)}, u32[]{:S(2)}) copy-start(s32[64]{0:T(128)S(1)} %get-tuple-element.19) | copy-start | bytes 772
  9.8 7.5 %copy-start.12 = (s32[64]{0:T(128)}, s32[64]{0:T(128)S(1)}, u32[]{:S(2)}) copy-start(s32[64]{0:T(128)S(1)} %get-tuple-element.18) | copy-start | bytes 772
  12.7 5.2 %copy-start.9 = (f32[2048]{0:T(1024)}, f32[2048]{0:T(1024)S(1)}, u32[]{:S(2)}) copy-start(f32[2048]{0:T(1024)S(1)} %convert_element_type.73) | copy-start | bytes 24580
  12.7 4.6 %copy-start.15 = (bf16[128]{0:T(256)(128)(2,1)S(1)}, bf16[128]{0:T(256)(128)(2,1)}, u32[]{:S(2)}) copy-start(bf16[128]{0:T(256)(128)(2,1)} %param.18) | copy-start | bytes 772
  12.7 5.2 %copy-start.1 = (bf16[256,2048]{1,0:T(8,128)(2,1)S(1)}, bf16[256,2048]{1,0:T(8,128)(2,1)}, u32[]{:S(2)}) copy-start(bf16[256,2048]{1,0:T(8,128)(2,1)} %param.10) | copy-start | bytes 3145732
  14.3 6.1 %copy-start.14 = (f32[256]{0:T(256)}, f32[256]{0:T(256)S(1)}, u32[]{:S(2)}) copy-start(f32[256]{0:T(256)S(1)} %add_rsqrt_fusion.2) | copy-start | bytes 3076
  22.6 0.6 copy-start.5
  25.6 3.5 %copy-start.16 = (bf16[128]{0:T(256)(128)(2,1)S(1)}, bf16[128]{0:T(256)(128)(2,1)}, u32[]{:S(2)}) copy-start(bf16[128]{0:T(256)(128)(2,1)} %param.17) | copy-start | bytes 772
  29.4 1.4 copy-start.4
  29.4 1.4 copy-start.8
  29.5 1.5 copy-start.2
  29.5 1.5 copy-start.3
  40.5 12.4 %copy-start.11 = (s32[64]{0:T(128)S(1)}, s32[64]{0:T(128)}, u32[]{:S(2)}) copy-start(s32[64]{0:T(128)} %copy-done.10) | copy-start | bytes 772
  40.5 15.0 %copy-start.13 = (s32[64]{0:T(128)S(1)}, s32[64]{0:T(128)}, u32[]{:S(2)}) copy-start(s32[64]{0:T(128)} %copy-done.12) | copy-start | bytes 772
  40.5 63.5 %all-to-all-start = ((bf16[16,64,1024]{2,0,1:T(8,128)(2,1)}), bf16[16,64,1024]{2,0,1:T(8,128)(2,1)}, u32[]{:S(2)}, u32[]{:S(2)}) async-start(bf16[16,64,1024]{2,0,1:T(8,128)(2,1)} %fusion.11), calls=%async_computation | async-start | bytes 4194304 | tf_op jit(solution)/shard_map/all_to_all | solution.py:118
  138.1 7.3 %copy-start.6 = (s32[256]{0:T(256)S(1)}, s32[256]{0:T(256)}, u32[]{:S(2)}) copy-start(s32[256]{0:T(256)} %copy-done.5) | copy-start | bytes 3076
  138.1 7.3 %copy-start.7 = (s32[256]{0:T(256)S(1)}, s32[256]{0:T(256)}, u32[]{:S(2)}) copy-start(s32[256]{0:T(256)} %get-tuple-element.16) | copy-start | bytes 3076
  139.7 34.3 %all-to-all-start.1 = ((bf16[16,64,512]{2,0,1:T(8,128)(2,1)}), bf16[16,64,512]{2,0,1:T(8,128)(2,1)}, u32[]{:S(2)}, u32[]{:S(2)}) async-start(bf16[16,64,512]{2,0,1:T(8,128)(2,1)} %copy.142), calls=%async_computation.1 | async-start | bytes 2097152 | tf_op jit(solution)/shard_map/all_to_all | solution.py:131
  145.3 55.9 %all-gather.2.cloned.1.call-start = ((), (), s32[]{:S(2)}) async-start(), calls=%async_computation.2 | async-start | bytes 1310720 | tf_op jit(solution)/shard_map/all_gather | solution.py:135
Sparse Core Ops, SparseCore 0:
  177.9 23.2 all-gather.1
where the time goes:
time: 213 us; the launch traced here: 212 us
  waiting for transfers between devices  95.7 us (45%)
  local copies, waits for them, and re-layouts  30.5 us (14%)
  matrix products  28.1 us (13%)
  other arithmetic  23.7 us (11%)
  starting transfers between devices  18 us (8%)
  between operations  16.4 us (8%)
    all_to_all x1, waiting for transfers between devices, on_device(): lax.all_to_all(jnp.where(send_valid[:, :, None], picked, jnp.zeros((), qk...  46 us
    all_to_all x1, waiting for transfers between devices, on_device(): lax.all_to_all(sendback, 'req', split_axis=1, concat_axis=1, tiled=True)  28.6 us
    all_gather x1, waiting for transfers between devices, on_device(): lax.all_gather(attended, 'tp', axis=1, tiled=True)  21.2 us
    all_to_all x1, starting transfers between devices, on_device(): lax.all_to_all(jnp.where(send_valid[:, :, None], picked, jnp.zeros((), qk...  12.4 us
    sub x1, matrix products, attend(): weights = jnp.exp(scores - row_max)  11.2 us
    dot_general x1, matrix products, attend(): jnp.einsum('kgqs,skd->qkgd', weights, values_split, preferred_element_typ...  7.24 us
    all_to_all x1, starting transfers between devices, on_device(): lax.all_to_all(sendback, 'req', split_axis=1, concat_axis=1, tiled=True)  5.63 us
    gather x1, local copies, waits for them, and re-layouts, on_device(): jnp.take(qkv_rows, send_rows, axis=0)  5.39 us
  transfers between devices with their start and end apart: 3, of which 3 were waited for; matrix products, arithmetic and copies ran while one was open for 3% of the time, Pallas kernels for 0%

commit v1 on v0

--- a/solution.py
+++ b/solution.py
@@ -74,6 +74,22 @@
 def on_device(
     hidden, lengths, dealing, norm_gain, w_query, w_key, w_value, query_gain, key_gain, w_out
 ):
+
+    def cover_indices(work_x):
+        count_all = lax.axis_size("tp")
+        vals = [(jj, (jj + 1) % count_all) for jj in range(count_all)]
+        block_list = [(jj, (jj - 1) % count_all) for jj in range(count_all)]
+        raw_out, tmp = ([work_x], [work_x])
+        for _ in range(count_all // 2):
+            f_next = lax.ppermute(raw_out[-1], "tp", vals)
+            raw_out.append(f_next)
+        for _ in range((count_all - 1) // 2):
+            val2 = lax.ppermute(tmp[-1], "tp", block_list)
+            tmp.append(val2)
+        long_array = jnp.concatenate([*raw_out[::-1], *tmp[1:]], axis=1)
+        next_value = lax.axis_index("tp")
+        return jnp.roll(long_array, (next_value - count_all // 2) * work_x.shape[1], axis=1)
+
     devices = lax.axis_size("req")
     home_index = lax.axis_index("req")
     slice_index = lax.axis_index("tp")
@@ -131,11 +147,7 @@
     returned = lax.all_to_all(sendback, "req", split_axis=1, concat_axis=1, tiled=True)
     attended = jnp.take(returned.reshape(capacity * devices, -1), back_rows, axis=0)
     kv_cache = jnp.stack([key_slot, value_slot])[:, None]
-    summed = jnp.dot(
-        lax.all_gather(attended, "tp", axis=1, tiled=True),
-        w_out,
-        preferred_element_type=jnp.float32,
-    )
+    summed = jnp.dot(cover_indices(attended), w_out, preferred_element_type=jnp.float32)
     branch = lax.optimization_barrier(summed.astype(jnp.bfloat16))
     residual = lax.dynamic_slice_in_dim(hidden, slice_index * out_width, out_width, 1)
     hidden_out = (residual.astype(jnp.float32) + branch.astype(jnp.float32)).astype(jnp.bfloat16)

time: 213 us -> 194 us (0.911); the launches traced: 212 us -> 191 us
  between operations: 16.4 us -> 3.09 us
  waiting for transfers between devices: 95.7 us -> 85 us
  starting transfers between devices: 18 us -> 22.9 us
    all_gather x1 -> x0, waiting for transfers between devices: 21.2 us -> none  [on_device(): lax.all_gather(attended, 'tp', axis=1, tiled=True)]
    ppermute x0 -> x3, waiting for transfers between devices: none -> 10.5 us  [the longest x2 8.85 us: cover_indices(): f_next = lax.ppermute(raw_out[-1], 'tp', vals)]
    ppermute x0 -> x3, starting transfers between devices: none -> 4.89 us  [the longest x1 2.93 us: cover_indices(): val2 = lax.ppermute(tmp[-1], 'tp', block_list)]
  transfers between devices with their start and end apart: 3 -> 5, of which waited for: 3 -> 5; matrix products, arithmetic and copies ran while one was open for 3% -> 3% of each run, Pallas kernels for 0% -> 0%
where the time goes in v1:
time: 194 us; the launch traced here: 191 us
  waiting for transfers between devices  85 us (44%)
  local copies, waits for them, and re-layouts  30.6 us (16%)
  matrix products  26.2 us (14%)
  other arithmetic  23.2 us (12%)
  starting transfers between devices  22.9 us (12%)
  between operations  3.09 us (2%)
    all_to_all x1, waiting for transfers between devices, on_device(): lax.all_to_all(jnp.where(send_valid[:, :, None], picked, jnp.zeros((), qk...  46 us
    all_to_all x1, waiting for transfers between devices, on_device(): lax.all_to_all(sendback, 'req', split_axis=1, concat_axis=1, tiled=True)  28.6 us
    all_to_all x1, starting transfers between devices, on_device(): lax.all_to_all(jnp.where(send_valid[:, :, None], picked, jnp.zeros((), qk...  12.4 us
    sub x1, matrix products, attend(): weights = jnp.exp(scores - row_max)  11.2 us
    ppermute x2, waiting for transfers between devices, cover_indices(): f_next = lax.ppermute(raw_out[-1], 'tp', vals)  8.85 us
    dot_general x1, matrix products, attend(): jnp.einsum('kgqs,skd->qkgd', weights, values_split, preferred_element_typ...  7.24 us
    all_to_all x1, starting transfers between devices, on_device(): lax.all_to_all(sendback, 'req', split_axis=1, concat_axis=1, tiled=True)  5.64 us
    gather x1, local copies, waits for them, and re-layouts, on_device(): jnp.take(qkv_rows, send_rows, axis=0)  5.39 us
  transfers between devices with their start and end apart: 5, of which 5 were waited for; matrix products, arithmetic and copies ran while one was open for 3% of the time, Pallas kernels for 0%

profile of v1, /device:TPU:2, one launch (start us, length us, event | category | flops | bytes accessed | tf_op | source)
XLA Modules:
  0.0 191.0 jit_solution(13377544485958813342)
XLA Ops:
  0.7 0.9 copy.123
  1.7 0.1 reduce
  1.8 0.7 sub.95
  2.4 0.8 select_reduce_fusion.2
  3.3 0.7 compare_select_fusion.7
  4.1 0.6 compare_and_fusion
  4.7 0.7 lt.134
  5.4 0.1 copy.124
  5.5 0.7 convert_element_type.73
  6.2 1.6 fusion.7
  7.8 2.2 %convolution_convert_fusion.1 = bf16[256,256]{0,1:T(8,128)(2,1)S(1)} fusion(bf16[2048,256]{1,0:T(8,128)(2,1)} %param.16, bf16[256,2048]{1,0:T(8,128)(2,1)} %param.10, f32[2048]{0:T(1024)S(1)} %convert_element_type.73, f32[256]{0:T(256)S(1)} %add_rsqrt_fusion.2), kind=kOutput, calls=%fused_computation.30 | convolution fusion | flops 270598144 | bytes 2237440 | tf_op jit(solution)/shard_map/dot_general | solution.py:42
  10.0 0.7 copy.131
  10.8 0.6 convert_element_type.79
  11.3 2.6 %multiply_reduce_fusion.1 = (f32[256,2]{0,1:T(2,128)S(1)}, f32[256,256]{0,1:T(8,128)}) fusion(bf16[2048,256]{1,0:T(8,128)(2,1)} %param.15, bf16[256,2048]{1,0:T(8,128)(2,1)S(1)} %copy-done.1, f32[2048]{0:T(1024)S(1)} %convert_element_type.73, f32[256]{0:T(256)S(1)} %add_rsqrt_fusion.2), kind=kOutput, calls=%fused_computation.43 | convolution fusion | flops 270663168 | bytes 2370560 | tf_op jit(solution)/shard_map/dot_general | solution.py:39
  13.9 0.6 add_rsqrt_fusion.1
  14.6 0.8 scatter_custom_fusion
  15.4 0.6 select_reduce_fusion
  16.0 0.6 copy-done.5
  16.6 0.3 multiply_cosine_fusion
  17.1 1.1 multiply_multiply_fusion.1
  18.3 0.8 copy.149
  19.0 2.3 %fusion.31 = f32[256,512]{1,0:T(8,128)} fusion(bf16[2048,512]{1,0:T(8,128)(2,1)S(1)} %copy-done, bf16[256,2048]{1,0:T(8,128)(2,1)S(1)} %copy-done.1, f32[2048]{0:T(1024)} %copy-done.9, f32[256]{0:T(256)} %copy-done.14), kind=kOutput, calls=%fused_computation.117 | convolution fusion | flops 538968064 | bytes 3679232 | tf_op jit(solution)/shard_map/dot_general | solution.py:36
  21.3 1.2 reshape.456
  22.5 0.3 multiply_reduce_fusion
  22.9 0.3 multiply_multiply_fusion
  23.3 0.5 subtract_convert_fusion
  23.8 0.4 pad_maximum_fusion.1
  24.4 0.1 copy.125
  24.5 5.4 %gather_fusion = bf16[1024,1024]{1,0:T(8,128)(2,1)} fusion(bf16[256,1024]{1,0:T(8,128)(2,1)S(1)} %pad_maximum_fusion, s32[1024]{0:T(1024)S(1)} %broadcast_clamp_fusion), kind=kCustom, calls=%fused_computation | custom fusion | bytes 4198400 | tf_op jit(solution)/shard_map/jit(_take)/gather | solution.py:133
  29.9 4.0 %fusion.11 = bf16[16,64,1024]{2,0,1:T(8,128)(2,1)} fusion(bf16[16,64,1024]{2,1,0:T(8,128)(2,1)} %bitcast.60, pred[16,64]{0,1:T(8,128)(4,1)S(1)} %copy.125, pred[16,64]{0,1:T(8,128)(4,1)S(1)} %copy.124), kind=kLoop, calls=%fused_computation.25 | loop fusion | flops 2097152 | bytes 4196352 | tf_op jit(solution)/shard_map/jit(_where)/select_n | solution.py:135
  34.0 12.4 %all-to-all-start = ((bf16[16,64,1024]{2,0,1:T(8,128)(2,1)}), bf16[16,64,1024]{2,0,1:T(8,128)(2,1)}, u32[]{:S(2)}, u32[]{:S(2)}) async-start(bf16[16,64,1024]{2,0,1:T(8,128)(2,1)} %fusion.11), calls=%async_computation | async-start | bytes 4194304 | tf_op jit(solution)/shard_map/all_to_all | solution.py:134
  46.4 0.6 dynamic_slice.23
  48.9 0.6 dynamic_slice.25
  49.5 0.6 iota_compare_fusion.3
  50.2 1.3 fusion.6
  51.5 46.0 %all-to-all-done = bf16[16,64,1024]{2,0,1:T(8,128)(2,1)} async-done(((bf16[16,64,1024]{2,0,1:T(8,128)(2,1)}), bf16[16,64,1024]{2,0,1:T(8,128)(2,1)}, u32[]{:S(2)}, u32[]{:S(2)}) %all-to-all-start) | async-done | bytes 2097184 | tf_op jit(solution)/shard_map/all_to_all | solution.py:134
  97.5 2.7 %copy.133 = bf16[16,64,1024]{2,1,0:T(8,128)(2,1)S(1)} copy(bf16[16,64,1024]{2,0,1:T(8,128)(2,1)} %all-to-all-done) | data formatting | bytes 4194304 | tf_op jit(solution)/shard_map/all_to_all | solution.py:134
  100.2 1.6 fusion.10
  101.8 1.4 slice_bitcast_fusion
  103.3 0.1 slice.38
  103.4 2.0 %copy.135 = bf16[1024,256]{0,1:T(8,128)(2,1)} copy(bf16[1024,256]{1,0:T(8,128)(2,1)} %get-tuple-element.23) | data formatting | bytes 1048576 | tf_op jit(solution)/shard_map/slice | solution.py:144
  105.4 2.1 %copy.136 = bf16[1024,256]{0,1:T(8,128)(2,1)} copy(bf16[1024,256]{1,0:T(8,128)(2,1)} %get-tuple-element.22) | data formatting | bytes 1048576 | tf_op jit(solution)/shard_map/slice | solution.py:143
  107.5 1.3 copy.137
  108.8 11.2 %fusion.33 = (f32[2,2,1024]{2,1,0:T(2,128)S(1)}, f32[2,2,1024,1024]{2,3,1,0:T(8,128)}) fusion(pred[1024,1024]{0,1:T(8,128)(4,1)} %fusion.6, bf16[1024,2,128,1]{0,2,3,1:T(8,128)(2,1)} %bitcast.67, bf16[1024,2,2,128]{0,3,2,1:T(8,128)(2,1)} %bitcast.64), kind=kOutput, calls=%fused_computation.118 | convolution fusion | flops 1090520064 | bytes 19415040 | tf_op jit(solution)/shard_map/sub | solution.py:66
  120.0 7.2 %fusion.15 = bf16[1024,2,2,128]{0,3,2,1:T(8,128)(2,1)S(1)} fusion(bf16[1024,2,128,1]{0,2,3,1:T(8,128)(2,1)} %bitcast.66, f32[2,2,1024,1024]{2,3,1,0:T(8,128)} %get-tuple-element.35, f32[2,2,1024]{2,1,0:T(2,128)S(1)} %get-tuple-element.34), kind=kOutput, calls=%fused_computation.28 | convolution fusion | flops 1082654720 | bytes 18366464 | tf_op jit(solution)/shard_map/kgqs,skd->qkgd/dot_general | solution.py:68
  127.3 2.0 %copy.141 = bf16[1024,2,2,128]{3,2,1,0:T(2,128)(2,1)} copy(bf16[1024,2,2,128]{0,3,2,1:T(8,128)(2,1)S(1)} %fusion.15) | data formatting | bytes 2097152 | tf_op jit(solution)/shard_map/convert_element_type | solution.py:71
  129.3 1.5 reshape_reshape.3
  130.8 0.8 fusion.16
  131.6 1.5 copy.142
  133.1 5.6 %all-to-all-start.1 = ((bf16[16,64,512]{2,0,1:T(8,128)(2,1)}), bf16[16,64,512]{2,0,1:T(8,128)(2,1)}, u32[]{:S(2)}, u32[]{:S(2)}) async-start(bf16[16,64,512]{2,0,1:T(8,128)(2,1)} %copy.142), calls=%async_computation.1 | async-start | bytes 2097152 | tf_op jit(solution)/shard_map/all_to_all | solution.py:147
  138.9 28.6 %all-to-all-done.1 = bf16[16,64,512]{2,0,1:T(8,128)(2,1)} async-done(((bf16[16,64,512]{2,0,1:T(8,128)(2,1)}), bf16[16,64,512]{2,0,1:T(8,128)(2,1)}, u32[]{:S(2)}, u32[]{:S(2)}) %all-to-all-start.1) | async-done | bytes 1048608 | tf_op jit(solution)/shard_map/all_to_all | solution.py:147
  167.5 1.8 copy.143
  169.3 1.2 gather_fusion.1
  170.5 1.7 collective-permute-start
  172.2 6.8 %collective-permute-done = bf16[256,512]{1,0:T(8,128)(2,1)S(1)} collective-permute-done((bf16[256,512]{1,0:T(8,128)(2,1)S(1)}, bf16[256,512]{1,0:T(8,128)(2,1)S(1)}, u32[]{:S(2)}, u32[]{:S(2)}) %collective-permute-start) | collective-permute-done | bytes 262176 | tf_op jit(solution)/shard_map/ppermute | solution.py:84
  178.9 0.3 collective-permute-start.1
  179.3 2.3 %maximum_bitcast_fusion = bf16[2,1,1024,256]{3,2,1,0:T(8,128)(2,1)} fusion(bf16[1,1024,256]{2,1,0:T(8,128)(2,1)} %get-tuple-element.21, bf16[1,1024,256]{2,1,0:T(8,128)(2,1)} %get-tuple-element.20), kind=kLoop, calls=%fused_computation.32 | loop fusion | flops 524288 | bytes 2097152
  181.5 2.9 %collective-permute-start.2 = (bf16[256,512]{1,0:T(8,128)(2,1)S(1)}, bf16[256,512]{1,0:T(8,128)(2,1)S(1)}, u32[]{:S(2)}, u32[]{:S(2)}) collective-permute-start(bf16[256,512]{1,0:T(8,128)(2,1)S(1)} %broadcast_select_fusion), channel_id=1, source_target_pairs={{0,3},{1,0},{2,1},{3,2},{4,7},{5,4},{6,5},{7,6},{8,11},{9,8},{10,9... | collective-permute-start | bytes 786440 | tf_op jit(solution)/shard_map/ppermute | solution.py:87
  184.5 2.1 %collective-permute-done.1 = bf16[256,512]{1,0:T(8,128)(2,1)S(1)} collective-permute-done((bf16[256,512]{1,0:T(8,128)(2,1)S(1)}, bf16[256,512]{1,0:T(8,128)(2,1)S(1)}, u32[]{:S(2)}, u32[]{:S(2)}) %collective-permute-start.1) | collective-permute-done | bytes 262176 | tf_op jit(solution)/shard_map/ppermute | solution.py:84
  186.6 0.1 constant_dynamic-update-slice_fusion.5
  186.7 1.6 collective-permute-done.2
  188.4 0.1 constant_dynamic-update-slice_fusion.1
  188.6 0.7 convolution_convert_fusion
  189.3 1.7 add_convert_fusion
  (65 shorter events, 1.1 us)
Async XLA Ops:
  0.6 18.4 %copy-start = (bf16[2048,512]{1,0:T(8,128)(2,1)S(1)}, bf16[2048,512]{1,0:T(8,128)(2,1)}, u32[]{:S(2)}) copy-start(bf16[2048,512]{1,0:T(8,128)(2,1)} %param.14) | copy-start | bytes 6291460
  3.3 2.2 %copy-start.10 = (s32[64]{0:T(128)}, s32[64]{0:T(128)S(1)}, u32[]{:S(2)}) copy-start(s32[64]{0:T(128)S(1)} %get-tuple-element.19) | copy-start | bytes 772
  3.3 7.5 %copy-start.12 = (s32[64]{0:T(128)}, s32[64]{0:T(128)S(1)}, u32[]{:S(2)}) copy-start(s32[64]{0:T(128)S(1)} %get-tuple-element.18) | copy-start | bytes 772
  6.2 5.2 %copy-start.9 = (f32[2048]{0:T(1024)}, f32[2048]{0:T(1024)S(1)}, u32[]{:S(2)}) copy-start(f32[2048]{0:T(1024)S(1)} %convert_element_type.73) | copy-start | bytes 24580
  6.2 4.6 %copy-start.16 = (bf16[128]{0:T(256)(128)(2,1)S(1)}, bf16[128]{0:T(256)(128)(2,1)}, u32[]{:S(2)}) copy-start(bf16[128]{0:T(256)(128)(2,1)} %param.18) | copy-start | bytes 772
  6.2 5.2 %copy-start.1 = (bf16[256,2048]{1,0:T(8,128)(2,1)S(1)}, bf16[256,2048]{1,0:T(8,128)(2,1)}, u32[]{:S(2)}) copy-start(bf16[256,2048]{1,0:T(8,128)(2,1)} %param.10) | copy-start | bytes 3145732
  7.8 6.1 %copy-start.14 = (f32[256]{0:T(256)}, f32[256]{0:T(256)S(1)}, u32[]{:S(2)}) copy-start(f32[256]{0:T(256)S(1)} %add_rsqrt_fusion.2) | copy-start | bytes 3076
  16.0 0.6 copy-start.5
  19.0 3.5 %copy-start.17 = (bf16[128]{0:T(256)(128)(2,1)S(1)}, bf16[128]{0:T(256)(128)(2,1)}, u32[]{:S(2)}) copy-start(bf16[128]{0:T(256)(128)(2,1)} %param.17) | copy-start | bytes 772
  22.9 1.4 copy-start.4
  22.9 1.4 copy-start.8
  22.9 1.5 copy-start.2
  22.9 1.5 copy-start.3
  34.0 12.4 %copy-start.11 = (s32[64]{0:T(128)S(1)}, s32[64]{0:T(128)}, u32[]{:S(2)}) copy-start(s32[64]{0:T(128)} %copy-done.10) | copy-start | bytes 772
  34.0 15.0 %copy-start.13 = (s32[64]{0:T(128)S(1)}, s32[64]{0:T(128)}, u32[]{:S(2)}) copy-start(s32[64]{0:T(128)} %copy-done.12) | copy-start | bytes 772
  34.0 63.5 %all-to-all-start = ((bf16[16,64,1024]{2,0,1:T(8,128)(2,1)}), bf16[16,64,1024]{2,0,1:T(8,128)(2,1)}, u32[]{:S(2)}, u32[]{:S(2)}) async-start(bf16[16,64,1024]{2,0,1:T(8,128)(2,1)} %fusion.11), calls=%async_computation | async-start | bytes 4194304 | tf_op jit(solution)/shard_map/all_to_all | solution.py:134
  131.6 7.2 %copy-start.6 = (s32[256]{0:T(256)S(1)}, s32[256]{0:T(256)}, u32[]{:S(2)}) copy-start(s32[256]{0:T(256)} %copy-done.5) | copy-start | bytes 3076
  131.6 7.2 %copy-start.7 = (s32[256]{0:T(256)S(1)}, s32[256]{0:T(256)}, u32[]{:S(2)}) copy-start(s32[256]{0:T(256)} %get-tuple-element.16) | copy-start | bytes 3076
  133.1 34.3 %all-to-all-start.1 = ((bf16[16,64,512]{2,0,1:T(8,128)(2,1)}), bf16[16,64,512]{2,0,1:T(8,128)(2,1)}, u32[]{:S(2)}, u32[]{:S(2)}) async-start(bf16[16,64,512]{2,0,1:T(8,128)(2,1)} %copy.142), calls=%async_computation.1 | async-start | bytes 2097152 | tf_op jit(solution)/shard_map/all_to_all | solution.py:147
  170.5 8.4 %collective-permute-start = (bf16[256,512]{1,0:T(8,128)(2,1)S(1)}, bf16[256,512]{1,0:T(8,128)(2,1)S(1)}, u32[]{:S(2)}, u32[]{:S(2)}) collective-permute-start(bf16[256,512]{1,0:T(8,128)(2,1)S(1)} %broadcast_select_fusion), channel_id=1, source_target_pairs={{0,1},{1,2},{2,3},{3,0},{4,5},{5,6},{6,7},{7,4},{8,9},{9,10},{10,1... | collective-permute-start | bytes 786440 | tf_op jit(solution)/shard_map/ppermute | solution.py:84
  178.9 7.6 %collective-permute-start.1 = (bf16[256,512]{1,0:T(8,128)(2,1)S(1)}, bf16[256,512]{1,0:T(8,128)(2,1)S(1)}, u32[]{:S(2)}, u32[]{:S(2)}) collective-permute-start(bf16[256,512]{1,0:T(8,128)(2,1)S(1)} %collective-permute-done), channel_id=1, source_target_pairs={{0,1},{1,2},{2,3},{3,0},{4,5},{5,6},{6,7},{7,4},{8,9},{9,10},{10,1... | collective-permute-start | bytes 786440 | tf_op jit(solution)/shard_map/ppermute | solution.py:84
  181.5 7.1 %copy-start.15 = (bf16[2048,512]{1,0:T(8,128)(2,1)S(1)}, bf16[2048,512]{1,0:T(8,128)(2,1)}, u32[]{:S(2)}) copy-start(bf16[2048,512]{1,0:T(8,128)(2,1)} %param.19) | copy-start | bytes 6291460
  181.5 6.8 %collective-permute-start.2 = (bf16[256,512]{1,0:T(8,128)(2,1)S(1)}, bf16[256,512]{1,0:T(8,128)(2,1)S(1)}, u32[]{:S(2)}, u32[]{:S(2)}) collective-permute-start(bf16[256,512]{1,0:T(8,128)(2,1)S(1)} %broadcast_select_fusion), channel_id=1, source_target_pairs={{0,3},{1,0},{2,1},{3,2},{4,7},{5,4},{6,5},{7,6},{8,11},{9,8},{10,9... | collective-permute-start | bytes 786440 | tf_op jit(solution)/shard_map/ppermute | solution.py:87
